TPU v7x, 128 devices: a whole 4x4x4 slice. The times are simulated.
128 devices in a mesh: sta: 2 (over x_lo), gx: 16 (over x_hi, z, core), gy: 4 (over y).
Axes of the slice: x: 4 (x_hi: 2, x_lo: 2; x = x_hi * 2 + x_lo), y: 4, z: 4, core: 2. Of those that a mesh axis runs over, the one named last changes fastest.
Arguments:
- record: float32 [128, 1024], replicated, may hold values from -6 to 6
- shifts: int32 [128, 256], P(None, 'gx'), may hold values from 0 to 1022
- station_group: int32 [128], replicated, may hold values from 0 to 7
- weights: bfloat16 [128, 256, 512], P('sta', 'gy'), may hold values from -6 to 6
- psf_real: float32 [256, 256, 512], P(None, 'gx', 'gy'), may hold values from -6 to 6
- psf_imag: float32 [256, 256, 512], P(None, 'gx', 'gy'), may hold values from -6 to 6
Outputs:
- image: float32 [2, 256, 256, 512], P('sta', 'gx', 'gy')
All inputs are finite; a program needn't handle non-finite values.
Results may differ from a plain program's by a relative error of at most 0.0029.
Values may be sent and summed in bfloat16 or wider, within the bound.
No kernel may reach another device: no remote copies, remote signals or barrier semaphores. Data moves between devices by JAX's collectives and lax.ppermute only.
A program may use at most 128 MiB of HBM per device.

v0:
```python
import math
import jax
import jax.numpy as jnp
from jax import lax
from jax.sharding import PartitionSpec as P

T_DEV = 1
NZ = 256
NX = 256
GROUPS = 8
NOISE_POWER = 0.25
HIGHEST = lax.Precision.HIGHEST


def station_counts(station_group):
    labels = jnp.arange(GROUPS, dtype=jnp.int32)
    onehot = (station_group[:, None] == labels[None, :]).astype(jnp.float32)
    totals = jnp.sum(onehot, axis=0)
    return jnp.dot(onehot, totals, precision=HIGHEST)


def coefficients(record, shifts, per_station, first_time, num_times):
    times_range = first_time + jnp.arange(num_times, dtype=jnp.int32)
    positions = shifts[:, :, None] + times_range[None, None, :]
    values = jnp.take_along_axis(record, positions.reshape(positions.shape[0], -1), axis=1)
    scaled = values.reshape(positions.shape) / per_station[:, None, None]
    return jnp.transpose(scaled, (2, 1, 0)).astype(jnp.bfloat16)


def fourier_parts(length, scale):
    indices = jnp.arange(length, dtype=jnp.int32)
    product = indices[:, None] * indices[None, :] % length
    angles = product.astype(jnp.float32) * (2.0 * math.pi / length)
    return (jnp.cos(angles) * scale, jnp.sin(angles) * scale)


def complex_table(length, forward):
    if forward:
        cosine, sine = fourier_parts(length, 1.0)
        return jnp.stack([jnp.stack([cosine, sine]), jnp.stack([-sine, cosine])])
    cosine, sine = fourier_parts(length, 1.0 / length)
    return jnp.stack([jnp.stack([cosine, -sine]), jnp.stack([sine, cosine])])


def along_rows(piece, table):
    return jnp.einsum("itzny,oikn->otzky", piece, table, precision=HIGHEST)


def along_depth(piece, table):
    return jnp.einsum("itnxy,oikn->otkxy", piece, table, precision=HIGHEST)


def on_device(record, shifts, station_group, weights, psf_real, psf_imag):
    per_station = station_counts(station_group)
    depth_rows = shifts.shape[1]
    lateral_rows = weights.shape[1]
    width_y = weights.shape[2]
    columns = lateral_rows * width_y
    first_time = lax.axis_index("sta") * T_DEV
    coefficient = coefficients(record, shifts, per_station, first_time, T_DEV)
    coefficient = coefficient.reshape(T_DEV * depth_rows, coefficient.shape[2])
    piece = lax.all_gather(weights, "sta", axis=0, tiled=True)
    stack = jnp.dot(
        coefficient, piece.reshape(piece.shape[0], columns), preferred_element_type=jnp.float32
    )
    stack = stack.reshape(T_DEV, depth_rows, lateral_rows, width_y)
    cosine_y, sine_y = fourier_parts(width_y, 1.0)
    spectrum = jnp.einsum(
        "tzxn,okn->otzxk", stack, jnp.stack([cosine_y, -sine_y]), precision=HIGHEST
    )
    row_table = complex_table(NX, True)
    by_rows = along_rows(
        lax.all_to_all(spectrum, "gy", split_axis=4, concat_axis=3, tiled=True), row_table
    )
    depth_table = complex_table(NZ, True)
    by_depth = along_depth(
        lax.all_to_all(by_rows, "gx", split_axis=3, concat_axis=2, tiled=True), depth_table
    )
    power = psf_real * psf_real + psf_imag * psf_imag + NOISE_POWER
    filt_real = (psf_real * by_depth[0] + psf_imag * by_depth[1]) / power
    filt_imag = (psf_real * by_depth[1] - psf_imag * by_depth[0]) / power
    back_depth = along_depth(jnp.stack([filt_real, filt_imag]), complex_table(NZ, False))
    back_table = complex_table(NX, False)
    back_rows = along_rows(
        lax.all_to_all(back_depth, "gx", split_axis=2, concat_axis=3, tiled=True), back_table
    )
    cosine_back, sine_back = fourier_parts(width_y, 1.0 / width_y)
    real_table = jnp.stack([cosine_back, -sine_back])
    return jnp.einsum(
        "itzxk,iyk->tzxy",
        lax.all_to_all(back_rows, "gy", split_axis=3, concat_axis=4, tiled=True),
        real_table,
        precision=HIGHEST,
    )


def solution(mesh):
    in_specs = (
        P(),
        P(None, "gx"),
        P(),
        P("sta", "gy", None),
        P(None, "gx", "gy"),
        P(None, "gx", "gy"),
    )
    out_specs = P("sta", "gx", "gy", None)
    return jax.shard_map(
        on_device, mesh=mesh, in_specs=in_specs, out_specs=out_specs, check_vma=False
    )
```

profile of v0, /device:TPU:0, one launch (start us, length us, event | category | flops | bytes accessed | tf_op | source)
XLA Modules:
  0.0 516.7 jit_solution(10342550417236700609)
XLA Ops:
  7.6 16.6 %gather_fusion = f32[2048]{0:T(1024)S(1)} fusion(f32[128,1024]{1,0:T(8,128)S(1)} %copy-done, s32[2048]{0:T(1024)S(1)} %reshape.275), kind=kCustom, calls=%fused_computation | custom fusion | bytes 32768 | tf_op jit(solution)/shard_map/jit(take_along_axis)/gather | solution.py:25
  28.7 89.3 %all-gather.2.cloned.1.call-done = bf16[128,64,512]{2,1,0:T(8,128)(2,1)} async-done(((bf16[64,64,512]{2,1,0:T(8,128)(2,1)}), bf16[128,64,512]{2,1,0:T(8,128)(2,1)}) %all-gather.2.cloned.1.call-update) | async-done | bytes 8388624 | tf_op jit(solution)/shard_map/all_gather | solution.py:62
  118.0 13.1 %copy.78 = bf16[128,64,512]{0,2,1:T(8,128)(2,1)} copy(bf16[128,64,512]{2,1,0:T(8,128)(2,1)} %all-gather.2.cloned.1.call-done) | data formatting | bytes 16777216 | tf_op jit(solution)/shard_map/reshape | solution.py:64
  131.1 5.8 %fusion = f32[16,64,512]{2,0,1:T(8,128)S(1)} fusion(bf16[128,64,512]{0,2,1:T(8,128)(2,1)} %copy.78, f32[128,16]{1,0:T(8,128)S(1)} %reshape.278, s32[128,16]{1,0:T(8,128)S(1)} %copy.50, f32[128]{0:T(128)S(1)} %convolution_bitcast_fusion.4, s32[]{:T(128)S(6)} %axis_index.15), kind=kOutput, calls=%fused_computation.1 | convolution fusion | flops 134238208 | bytes 10502660 | tf_op jit(solution)/shard_map/dot_general | solution.py:63
  136.9 9.2 %convolution_bitcast_fusion = f32[2,1,16,64,512]{4,3,2,0,1:T(8,128)} fusion(f32[1,512,512]{2,1,0:T(8,128)S(1)} %get-tuple-element.12, f32[1,512,512]{2,1,0:T(8,128)S(1)} %get-tuple-element.11, f32[16,64,512]{2,0,1:T(8,128)S(1)} %fusion), kind=kOutput, calls=%fused_computation.8 | convolution fusion | flops 6442975232 | bytes 8388608 | tf_op jit(solution)/shard_map/tzxn,okn->otzxk/dot_general | solution.py:68
  146.0 9.1 %copy.54 = f32[2,1,16,64,512]{3,2,0,1,4:T(8,128)} copy(f32[2,1,16,64,512]{4,3,2,0,1:T(8,128)} %convolution_bitcast_fusion) | data formatting | bytes 8388608 | tf_op jit(solution)/shard_map/tzxn,okn->otzxk/transpose | solution.py:68
  155.2 19.9 %reshape.303 = f32[4,1,262144]{2,1,0:T(1,128)} reshape(f32[512,1,2,16,64]{4,3,2,1,0:T(8,128)} %bitcast.153) | data formatting | bytes 8388608
  175.1 4.8 all-to-all-start
  182.1 47.0 %all-to-all-done = f32[4,1,262144]{2,1,0:T(1,128)} async-done(((f32[4,1,262144]{2,1,0:T(1,128)}), f32[4,1,262144]{2,1,0:T(1,128)}, u32[]{:S(2)}, u32[]{:S(2)}) %all-to-all-start) | async-done | bytes 4194336 | tf_op jit(solution)/shard_map/all_to_all | solution.py:73
  229.6 15.2 %reduce = f32[4,262144]{1,0:T(4,128)} reduce(f32[4,1,262144]{2,1,0:T(1,128)} %all-to-all-done, f32[]{:T(128)} %broadcast.479), dimensions={1}, to_apply=%all_to_all.44.reduce_sub_computation | reduce | bytes 8388612 | tf_op jit(solution)/shard_map/all_to_all | solution.py:73
  244.8 9.3 %reshape.304 = f32[512,1,2,16,64]{4,3,2,1,0:T(8,128)} reshape(f32[4,262144]{1,0:T(4,128)} %reduce) | data formatting | bytes 8388608
  254.1 6.9 %copy.55 = f32[2,1,16,64,4,128]{5,3,4,0,2,1:T(8,128)} copy(f32[2,1,16,64,4,128]{3,2,0,5,4,1:T(8,128)} %bitcast.154) | data formatting | bytes 8388608 | tf_op jit(solution)/shard_map/all_to_all | solution.py:73
  261.0 8.7 %convolution_bitcast_fusion.3 = f32[2,1,16,256,128]{4,3,2,0,1:T(8,128)S(1)} fusion(f32[2,16,256,128,1]{3,2,0,1,4:T(8,128)} %bitcast.155, f32[1,2,256,256]{3,2,1,0:T(8,128)S(1)} %get-tuple-element.10, f32[1,2,256,256]{3,2,1,0:T(8,128)S(1)} %get-tuple-element.9), kind=kOutput, calls=%fused_computation.12 | convolution fusion | flops 6442713088 | bytes 9437184 | tf_op jit(solution)/shard_map/itzny,oikn->otzky/dot_general | solution.py:46
  274.1 6.9 %all-to-all-start.1 = ((f32[2,1,16,256,128]{4,2,0,1,3:T(8,128)}), f32[2,1,16,256,128]{4,2,0,1,3:T(8,128)}, u32[]{:S(2)}, u32[]{:S(2)}) async-start(f32[2,1,16,256,128]{4,2,0,1,3:T(8,128)} %copy.56), calls=%async_computation.1 | async-start | bytes 8388608 | tf_op jit(solution)/shard_map/all_to_all | solution.py:77
  283.1 53.2 %all-to-all-done.1 = f32[2,1,16,256,128]{4,2,0,1,3:T(8,128)} async-done(((f32[2,1,16,256,128]{4,2,0,1,3:T(8,128)}), f32[2,1,16,256,128]{4,2,0,1,3:T(8,128)}, u32[]{:S(2)}, u32[]{:S(2)}) %all-to-all-start.1) | async-done | bytes 4194336 | tf_op jit(solution)/shard_map/all_to_all | solution.py:77
  339.1 7.1 %convolution_bitcast_fusion.2 = f32[2,256,16,128]{3,1,2,0:T(8,128)S(1)} fusion(f32[2,256,16,128,1]{3,1,0,2,4:T(8,128)S(1)} %bitcast.157, f32[1,2,256,256]{3,2,1,0:T(8,128)S(1)} %get-tuple-element.10, f32[1,2,256,256]{3,2,1,0:T(8,128)S(1)} %get-tuple-element.9), kind=kOutput, calls=%fused_computation.11 | convolution fusion | flops 6442713088 | bytes 9437184 | tf_op jit(solution)/shard_map/itnxy,oikn->otkxy/dot_general | solution.py:50
  347.7 7.3 %fusion.5 = f32[2,1,256,16,128]{4,2,3,0,1:T(8,128)S(1)} fusion(f32[1,2,256,256]{3,2,1,0:T(8,128)S(1)} %get-tuple-element.8, f32[1,2,256,256]{3,2,1,0:T(8,128)S(1)} %get-tuple-element.7, f32[1,1,256,16,128]{4,2,3,1,0:T(8,128)S(1)} %get-tuple-element.6, f32[1,1,256,16,128]{4,2,3,1,0:T(8,128)S(1)} %get-tuple-element.5), kind=kOutput, calls=%fused_computation.9 | convolution fusion | flops 6443761664 | bytes 9437184 | tf_op jit(solution)/shard_map/itnxy,oikn->otkxy/dot_general | solution.py:50
  357.5 64.3 %all_to_all.60 = f32[2,1,256,16,128]{4,3,0,1,2:T(8,128)S(1)} all-to-all(f32[2,1,256,16,128]{4,3,0,1,2:T(8,128)S(1)} %copy.64), channel_id=1, replica_groups=mesh['sta'=2,'gx'=16,'gy'=4] {'gx'}, dimensions={2} | all-to-all | bytes 8388608 | tf_op jit(solution)/shard_map/all_to_all | solution.py:85
  422.3 6.9 %convolution_bitcast_fusion.1 = f32[2,1,16,256,128]{4,3,2,0,1:T(8,128)S(1)} fusion(f32[2,16,256,128,1]{3,2,0,1,4:T(8,128)S(1)} %bitcast.156, f32[1,2,256,256]{3,2,1,0:T(8,128)S(1)} %get-tuple-element.8, f32[1,2,256,256]{3,2,1,0:T(8,128)S(1)} %get-tuple-element.7), kind=kOutput, calls=%fused_computation.10 | convolution fusion | flops 6442713088 | bytes 9437184 | tf_op jit(solution)/shard_map/itzny,oikn->otzky/dot_general | solution.py:46
  433.6 5.1 all-to-all-start.3
  442.8 44.5 %all-to-all-done.3 = f32[2,1,16,256,128]{4,2,0,1,3:T(8,128)} async-done(((f32[2,1,16,256,128]{4,2,0,1,3:T(8,128)}), f32[2,1,16,256,128]{4,2,0,1,3:T(8,128)}, u32[]{:S(2)}, u32[]{:S(2)}) %all-to-all-start.3) | async-done | bytes 4194336 | tf_op jit(solution)/shard_map/all_to_all | solution.py:91
  487.3 6.9 %copy.94 = f32[2,1,16,4,64,128]{5,3,4,0,2,1:T(4,128)} copy(f32[2,1,16,4,64,128]{5,2,0,4,3,1:T(8,128)} %bitcast.57) | data formatting | bytes 8388608 | tf_op jit(solution)/shard_map/all_to_all | solution.py:91
  494.2 5.5 %reshape.274 = f32[2,16,64,512]{3,2,0,1:T(8,128)} reshape(f32[2,1,16,64,4,128]{5,4,3,0,2,1:T(4,128)} %bitcast.159) | data formatting | bytes 8388608 | tf_op jit(solution)/shard_map/reshape.27
  499.7 9.9 %fusion.19 = f32[1,16,64,512]{3,2,1,0:T(8,128)} fusion(f32[2,16,64,512]{3,2,0,1:T(8,128)} %reshape.274, f32[1,512,512]{2,1,0:T(8,128)S(1)} %get-tuple-element.17, f32[1,512,512]{2,1,0:T(8,128)S(1)} %get-tuple-element.18), kind=kOutput, calls=%fused_computation.33 | convolution fusion | flops 6442975232 | bytes 8388608 | tf_op jit(solution)/shard_map/itzxk,iyk->tzxy/dot_general | solution.py:89
  (35 shorter events, 30.4 us)
Async XLA Ops:
  6.5 1.1 copy-start
  6.5 0.8 copy-start.4
  6.5 111.5 %all-gather.2.cloned.1.call-start = ((), (), s32[]{:S(2)}) async-start(), calls=%async_computation.4 | async-start | bytes 12582912 | tf_op jit(solution)/shard_map/all_gather | solution.py:62
  7.6 16.7 %copy-start.5 = (s32[128]{0:T(128)S(1)}, s32[128]{0:T(128)}, u32[]{:S(2)}) copy-start(s32[128]{0:T(128)} %param.8) | copy-start | bytes 1540
  175.1 54.0 %all-to-all-start = ((f32[4,1,262144]{2,1,0:T(1,128)}), f32[4,1,262144]{2,1,0:T(1,128)}, u32[]{:S(2)}, u32[]{:S(2)}) async-start(f32[4,1,262144]{2,1,0:T(1,128)} %reshape.303), calls=%async_computation | async-start | bytes 8388608 | tf_op jit(solution)/shard_map/all_to_all | solution.py:73
  274.1 62.2 %all-to-all-start.1 = ((f32[2,1,16,256,128]{4,2,0,1,3:T(8,128)}), f32[2,1,16,256,128]{4,2,0,1,3:T(8,128)}, u32[]{:S(2)}, u32[]{:S(2)}) async-start(f32[2,1,16,256,128]{4,2,0,1,3:T(8,128)} %copy.56), calls=%async_computation.1 | async-start | bytes 8388608 | tf_op jit(solution)/shard_map/all_to_all | solution.py:77
  339.0 7.2 %copy-start.2 = (f32[256,16,128]{2,1,0:T(8,128)S(1)}, f32[256,16,128]{2,1,0:T(8,128)}, u32[]{:S(2)}) copy-start(f32[256,16,128]{2,1,0:T(8,128)} %param.11) | copy-start | bytes 6291460
  339.0 7.2 %copy-start.3 = (f32[256,16,128]{2,1,0:T(8,128)S(1)}, f32[256,16,128]{2,1,0:T(8,128)}, u32[]{:S(2)}) copy-start(f32[256,16,128]{2,1,0:T(8,128)} %param.10) | copy-start | bytes 6291460
  433.6 53.7 %all-to-all-start.3 = ((f32[2,1,16,256,128]{4,2,0,1,3:T(8,128)}), f32[2,1,16,256,128]{4,2,0,1,3:T(8,128)}, u32[]{:S(2)}, u32[]{:S(2)}) async-start(f32[2,1,16,256,128]{4,2,0,1,3:T(8,128)} %copy.66), calls=%async_computation.3 | async-start | bytes 8388608 | tf_op jit(solution)/shard_map/all_to_all | solution.py:91
  499.7 9.9 %copy-start.1 = (f32[128,1024]{1,0:T(8,128)S(1)}, f32[128,1024]{1,0:T(8,128)}, u32[]{:S(2)}) copy-start(f32[128,1024]{1,0:T(8,128)} %param.6) | copy-start | bytes 1572868
Sparse Core Ops, SparseCore 0:
  9.0 108.9 all-gather.1
where the time goes:
time: 526 us; the launch traced here: 517 us
  waiting for transfers between devices  235 us (45%)
  local copies, waits for them, and re-layouts  103 us (20%)
  blocking collectives  64.3 us (12%)
  matrix products  55 us (10%)
  other arithmetic  29.4 us (6%)
  starting transfers between devices  16.8 us (3%)
  between operations  13.8 us (3%)
    all_gather x1, waiting for transfers between devices, on_device(): piece = lax.all_gather(weights, 'sta', axis=0, tiled=True)  89.3 us
    all_to_all x1, blocking collectives, on_device(): lax.all_to_all(back_depth, 'gx', split_axis=2, concat_axis=3, tiled=True)  64.3 us
    all_to_all x1, waiting for transfers between devices, on_device(): lax.all_to_all(by_rows, 'gx', split_axis=3, concat_axis=2, tiled=True)  53.2 us
    all_to_all x1, waiting for transfers between devices, on_device(): lax.all_to_all(spectrum, 'gy', split_axis=4, concat_axis=3, tiled=True)  47 us
    all_to_all x1, waiting for transfers between devices, on_device(): lax.all_to_all(back_rows, 'gy', split_axis=3, concat_axis=4, tiled=True)  44.5 us
    unnamed x15, local copies, waits for them, and re-layouts  29.4 us
    gather x3, local copies, waits for them, and re-layouts, coefficients(): jnp.take_along_axis(record, positions.reshape(positions.shape[0], -1), ax...  16.8 us
    dot_general x2, matrix products, along_rows(): return jnp.einsum('itzny,oikn->otzky', piece, table, precision=HIGHEST)  15.6 us
  transfers between devices with their start and end apart: 4, of which 4 were waited for; matrix products, arithmetic and copies ran while one was open for 6% of the time, Pallas kernels for 0%

commit v1 on v0

--- a/solution.py
+++ b/solution.py
@@ -59,7 +59,8 @@
     first_time = lax.axis_index("sta") * T_DEV
     coefficient = coefficients(record, shifts, per_station, first_time, T_DEV)
     coefficient = coefficient.reshape(T_DEV * depth_rows, coefficient.shape[2])
-    piece = lax.all_gather(weights, "sta", axis=0, tiled=True)
+    sent = jnp.stack([weights] * lax.axis_size("sta"))
+    piece = jnp.concatenate(lax.all_to_all(sent, "sta", 0, 0), axis=0)
     stack = jnp.dot(
         coefficient, piece.reshape(piece.shape[0], columns), preferred_element_type=jnp.float32
     )

time: 526 us -> 510 us (0.970)
  waiting for transfers between devices: 235 us -> 215 us
  between operations: 13.8 us -> 0.47 us
  starting transfers between devices: 16.8 us -> 25.4 us
  other arithmetic: 29.4 us -> 36.9 us
    all_gather x1 -> x0, waiting for transfers between devices: 89.3 us -> none  [on_device(): piece = lax.all_gather(weights, 'sta', axis=0, tiled=True)]
    all_to_all x0 -> x1, waiting for transfers between devices: none -> 71.1 us  [on_device(): piece = jnp.concatenate(lax.all_to_all(sent, 'sta', 0, 0), axis=0)]
    reshape x1 -> x0, local copies, waits for them, and re-layouts: 13.1 us -> none  [on_device(): piece.reshape(piece.shape[0], columns)]
    another operation x1 -> x2, local copies, waits for them, and re-layouts: 5.49 us -> 17.9 us  [the longest x1 12.4 us: on_device(): piece.reshape(piece.shape[0], columns)]
    another operation x0 -> x1, other arithmetic: none -> 7.51 us  [on_device(): sent = jnp.stack([weights] * lax.axis_size('sta'))]
    all_to_all x0 -> x1, starting transfers between devices: none -> 7.08 us  [on_device(): piece = jnp.concatenate(lax.all_to_all(sent, 'sta', 0, 0), axis=0)]
    unnamed x15 -> x16, local copies, waits for them, and re-layouts: 29.4 us -> 30.5 us
where the time goes in v1:
time: 510 us; the launch traced here: 500 us
  waiting for transfers between devices  215 us (42%)
  local copies, waits for them, and re-layouts  103 us (20%)
  blocking collectives  64.3 us (13%)
  matrix products  55.3 us (11%)
  other arithmetic  36.9 us (7%)
  starting transfers between devices  25.4 us (5%)
    all_to_all x1, waiting for transfers between devices, on_device(): piece = jnp.concatenate(lax.all_to_all(sent, 'sta', 0, 0), axis=0)  71.1 us
    all_to_all x1, blocking collectives, on_device(): lax.all_to_all(back_depth, 'gx', split_axis=2, concat_axis=3, tiled=True)  64.3 us
    all_to_all x1, waiting for transfers between devices, on_device(): lax.all_to_all(by_rows, 'gx', split_axis=3, concat_axis=2, tiled=True)  53.1 us
    all_to_all x1, waiting for transfers between devices, on_device(): lax.all_to_all(spectrum, 'gy', split_axis=4, concat_axis=3, tiled=True)  46.3 us
    all_to_all x1, waiting for transfers between devices, on_device(): lax.all_to_all(back_rows, 'gy', split_axis=3, concat_axis=4, tiled=True)  44.5 us
    unnamed x16, local copies, waits for them, and re-layouts  30.5 us
    gather x3, local copies, waits for them, and re-layouts, coefficients(): jnp.take_along_axis(record, positions.reshape(positions.shape[0], -1), ax...  16.8 us
    dot_general x2, matrix products, along_rows(): return jnp.einsum('itzny,oikn->otzky', piece, table, precision=HIGHEST)  15.8 us
  transfers between devices with their start and end apart: 4, of which 4 were waited for; matrix products, arithmetic and copies ran while one was open for 6% of the time, Pallas kernels for 0%

profile of v1, /device:TPU:0, one launch (start us, length us, event | category | flops | bytes accessed | tf_op | source)
XLA Modules:
  0.0 500.3 jit_solution(15269633654173231328)
XLA Ops:
  0.0 7.5 %pad_maximum_fusion = bf16[2,64,64,512]{3,2,1,0:T(8,128)(2,1)} fusion(bf16[1,64,64,512]{3,2,1,0:T(8,128)(2,1)} %bitcast.163), kind=kLoop, calls=%fused_computation.1 | loop fusion | flops 4194304 | bytes 12582912 | tf_op jit(solution)/shard_map/stack | solution.py:62
  7.5 7.1 %all-to-all-start = ((bf16[2,64,64,512]{3,2,1,0:T(8,128)(2,1)}), bf16[2,64,64,512]{3,2,1,0:T(8,128)(2,1)}, u32[]{:S(2)}, u32[]{:S(2)}) async-start(bf16[2,64,64,512]{3,2,1,0:T(8,128)(2,1)} %pad_maximum_fusion), calls=%async_computation | async-start | bytes 16777216 | tf_op jit(solution)/shard_map/all_to_all | solution.py:63
  14.9 16.6 %gather_fusion = f32[2048]{0:T(1024)S(1)} fusion(f32[128,1024]{1,0:T(8,128)S(1)} %copy-done, s32[2048]{0:T(1024)S(1)} %reshape.271), kind=kCustom, calls=%fused_computation | custom fusion | bytes 32768 | tf_op jit(solution)/shard_map/jit(take_along_axis)/gather | solution.py:25
  36.0 71.1 %all-to-all-done = bf16[2,64,64,512]{3,2,1,0:T(8,128)(2,1)} async-done(((bf16[2,64,64,512]{3,2,1,0:T(8,128)(2,1)}), bf16[2,64,64,512]{3,2,1,0:T(8,128)(2,1)}, u32[]{:S(2)}, u32[]{:S(2)}) %all-to-all-start) | async-done | bytes 8388640 | tf_op jit(solution)/shard_map/all_to_all | solution.py:63
  107.1 12.5 %copy.78 = bf16[16,8,64,512]{3,1,2,0:T(8,128)(2,1)} copy(bf16[16,8,64,512]{3,2,1,0:T(8,128)(2,1)} %bitcast.79) | data formatting | bytes 16777216
  119.5 12.4 %copy.51 = bf16[128,32768]{0,1:T(8,128)(2,1)} copy(bf16[128,32768]{1,0:T(8,128)(2,1)} %bitcast.157) | data formatting | bytes 16777216 | tf_op jit(solution)/shard_map/reshape;reshape | solution.py:65
  131.9 5.8 %fusion.37 = f32[16,64,512]{2,0,1:T(8,128)S(1)} fusion(bf16[64,512,128]{2,1,0:T(8,128)(2,1)} %bitcast.156, f32[128,16]{1,0:T(8,128)S(1)} %reshape.274, s32[128,16]{1,0:T(8,128)S(1)} %copy.50, f32[128]{0:T(128)S(1)} %convolution_bitcast_fusion.4, s32[]{:T(128)S(6)} %axis_index.15), kind=kOutput, calls=%fused_computation.72 | convolution fusion | flops 134238208 | bytes 10502660 | tf_op jit(solution)/shard_map/dot_general | solution.py:64
  137.7 9.1 %convolution_bitcast_fusion = f32[2,1,16,64,512]{4,3,2,0,1:T(8,128)} fusion(f32[1,512,512]{2,1,0:T(8,128)S(1)} %get-tuple-element.12, f32[1,512,512]{2,1,0:T(8,128)S(1)} %get-tuple-element.11, f32[16,64,512]{2,0,1:T(8,128)S(1)} %fusion.37), kind=kOutput, calls=%fused_computation.7 | convolution fusion | flops 6442975232 | bytes 8388608 | tf_op jit(solution)/shard_map/tzxn,okn->otzxk/dot_general | solution.py:69
  146.8 9.1 %copy.54 = f32[2,1,16,64,512]{3,2,0,1,4:T(8,128)} copy(f32[2,1,16,64,512]{4,3,2,0,1:T(8,128)} %convolution_bitcast_fusion) | data formatting | bytes 8388608 | tf_op jit(solution)/shard_map/tzxn,okn->otzxk/transpose | solution.py:69
  155.9 8.6 %reshape.299 = f32[4,1,262144]{2,1,0:T(1,128)} reshape(f32[512,1,2,16,64]{4,3,2,1,0:T(8,128)} %bitcast.154) | data formatting | bytes 8388608
  171.7 46.3 %all-to-all-done.1 = f32[4,1,262144]{2,1,0:T(1,128)} async-done(((f32[4,1,262144]{2,1,0:T(1,128)}), f32[4,1,262144]{2,1,0:T(1,128)}, u32[]{:S(2)}, u32[]{:S(2)}) %all-to-all-start.1) | async-done | bytes 4194336 | tf_op jit(solution)/shard_map/all_to_all | solution.py:74
  218.6 15.2 %reduce = f32[4,262144]{1,0:T(4,128)} reduce(f32[4,1,262144]{2,1,0:T(1,128)} %all-to-all-done.1, f32[]{:T(128)} %broadcast.479), dimensions={1}, to_apply=%all_to_all.48.reduce_sub_computation | reduce | bytes 8388612 | tf_op jit(solution)/shard_map/all_to_all | solution.py:74
  233.8 9.3 %reshape.300 = f32[512,1,2,16,64]{4,3,2,1,0:T(8,128)} reshape(f32[4,262144]{1,0:T(4,128)} %reduce) | data formatting | bytes 8388608
  243.0 6.8 %copy.55 = f32[2,1,16,64,4,128]{5,3,4,0,2,1:T(8,128)} copy(f32[2,1,16,64,4,128]{3,2,0,5,4,1:T(8,128)} %bitcast.155) | data formatting | bytes 8388608 | tf_op jit(solution)/shard_map/all_to_all | solution.py:74
  249.9 8.9 %convolution_bitcast_fusion.3 = f32[2,1,16,256,128]{4,3,2,0,1:T(8,128)S(1)} fusion(f32[2,16,256,128,1]{3,2,0,1,4:T(8,128)} %bitcast.158, f32[1,2,256,256]{3,2,1,0:T(8,128)S(1)} %get-tuple-element.10, f32[1,2,256,256]{3,2,1,0:T(8,128)S(1)} %get-tuple-element.9), kind=kOutput, calls=%fused_computation.11 | convolution fusion | flops 6442713088 | bytes 9437184 | tf_op jit(solution)/shard_map/itzny,oikn->otzky/dot_general | solution.py:46
  263.2 8.2 %all-to-all-start.2 = ((f32[2,1,16,256,128]{4,2,0,1,3:T(8,128)}), f32[2,1,16,256,128]{4,2,0,1,3:T(8,128)}, u32[]{:S(2)}, u32[]{:S(2)}) async-start(f32[2,1,16,256,128]{4,2,0,1,3:T(8,128)} %copy.56), calls=%async_computation.2 | async-start | bytes 8388608 | tf_op jit(solution)/shard_map/all_to_all | solution.py:78
  273.6 53.1 %all-to-all-done.2 = f32[2,1,16,256,128]{4,2,0,1,3:T(8,128)} async-done(((f32[2,1,16,256,128]{4,2,0,1,3:T(8,128)}), f32[2,1,16,256,128]{4,2,0,1,3:T(8,128)}, u32[]{:S(2)}, u32[]{:S(2)}) %all-to-all-start.2) | async-done | bytes 4194336 | tf_op jit(solution)/shard_map/all_to_all | solution.py:78
  329.4 7.1 %convolution_bitcast_fusion.2 = f32[2,256,16,128]{3,1,2,0:T(8,128)S(1)} fusion(f32[2,256,16,128,1]{3,1,0,2,4:T(8,128)S(1)} %bitcast.160, f32[1,2,256,256]{3,2,1,0:T(8,128)S(1)} %get-tuple-element.10, f32[1,2,256,256]{3,2,1,0:T(8,128)S(1)} %get-tuple-element.9), kind=kOutput, calls=%fused_computation.10 | convolution fusion | flops 6442713088 | bytes 9437184 | tf_op jit(solution)/shard_map/itnxy,oikn->otkxy/dot_general | solution.py:50
  338.1 7.4 %fusion.3 = f32[2,1,256,16,128]{4,2,3,0,1:T(8,128)S(1)} fusion(f32[1,2,256,256]{3,2,1,0:T(8,128)S(1)} %get-tuple-element.8, f32[1,2,256,256]{3,2,1,0:T(8,128)S(1)} %get-tuple-element.7, f32[1,1,256,16,128]{4,2,3,1,0:T(8,128)S(1)} %get-tuple-element.6, f32[1,1,256,16,128]{4,2,3,1,0:T(8,128)S(1)} %get-tuple-element.5), kind=kOutput, calls=%fused_computation.8 | convolution fusion | flops 6443761664 | bytes 9437184 | tf_op jit(solution)/shard_map/itnxy,oikn->otkxy/dot_general | solution.py:50
  347.9 64.3 %all_to_all.65 = f32[2,1,256,16,128]{4,3,0,1,2:T(8,128)S(1)} all-to-all(f32[2,1,256,16,128]{4,3,0,1,2:T(8,128)S(1)} %copy.64), channel_id=1, replica_groups=mesh['sta'=2,'gx'=16,'gy'=4] {'gx'}, dimensions={2} | all-to-all | bytes 8388608 | tf_op jit(solution)/shard_map/all_to_all | solution.py:86
  412.8 6.9 %convolution_bitcast_fusion.1 = f32[2,1,16,256,128]{4,3,2,0,1:T(8,128)S(1)} fusion(f32[2,16,256,128,1]{3,2,0,1,4:T(8,128)S(1)} %bitcast.159, f32[1,2,256,256]{3,2,1,0:T(8,128)S(1)} %get-tuple-element.8, f32[1,2,256,256]{3,2,1,0:T(8,128)S(1)} %get-tuple-element.7), kind=kOutput, calls=%fused_computation.9 | convolution fusion | flops 6442713088 | bytes 9437184 | tf_op jit(solution)/shard_map/itzny,oikn->otzky/dot_general | solution.py:46
  433.3 44.5 %all-to-all-done.4 = f32[2,1,16,256,128]{4,2,0,1,3:T(8,128)} async-done(((f32[2,1,16,256,128]{4,2,0,1,3:T(8,128)}), f32[2,1,16,256,128]{4,2,0,1,3:T(8,128)}, u32[]{:S(2)}, u32[]{:S(2)}) %all-to-all-start.4) | async-done | bytes 4194336 | tf_op jit(solution)/shard_map/all_to_all | solution.py:92
  477.7 6.8 %copy.94 = f32[2,1,16,4,64,128]{5,3,4,0,2,1:T(4,128)} copy(f32[2,1,16,4,64,128]{5,2,0,4,3,1:T(8,128)} %bitcast.57) | data formatting | bytes 8388608 | tf_op jit(solution)/shard_map/all_to_all | solution.py:92
  490.1 9.9 %fusion.17 = f32[1,16,64,512]{3,2,1,0:T(8,128)} fusion(f32[2,16,64,512]{3,2,0,1:T(8,128)} %reshape.270, f32[1,512,512]{2,1,0:T(8,128)S(1)} %get-tuple-element.17, f32[1,512,512]{2,1,0:T(8,128)S(1)} %get-tuple-element.18), kind=kOutput, calls=%fused_computation.32 | convolution fusion | flops 6442975232 | bytes 8388608 | tf_op jit(solution)/shard_map/itzxk,iyk->tzxy/dot_general | solution.py:90
  (36 shorter events, 45.1 us)
Async XLA Ops:
  0.0 14.8 %copy-start = (f32[128,1024]{1,0:T(8,128)S(1)}, f32[128,1024]{1,0:T(8,128)}, u32[]{:S(2)}) copy-start(f32[128,1024]{1,0:T(8,128)} %param.6) | copy-start | bytes 1572868
  7.5 7.1 %copy-start.4 = (s32[128,16]{0,1:T(8,128)S(1)}, s32[128,16]{0,1:T(8,128)}, u32[]{:S(2)}) copy-start(s32[128,16]{0,1:T(8,128)} %param.7) | copy-start | bytes 24580
  7.5 99.5 %all-to-all-start = ((bf16[2,64,64,512]{3,2,1,0:T(8,128)(2,1)}), bf16[2,64,64,512]{3,2,1,0:T(8,128)(2,1)}, u32[]{:S(2)}, u32[]{:S(2)}) async-start(bf16[2,64,64,512]{3,2,1,0:T(8,128)(2,1)} %pad_maximum_fusion), calls=%async_computation | async-start | bytes 16777216 | tf_op jit(solution)/shard_map/all_to_all | solution.py:63
  14.8 16.8 %copy-start.5 = (s32[128]{0:T(128)S(1)}, s32[128]{0:T(128)}, u32[]{:S(2)}) copy-start(s32[128]{0:T(128)} %param.8) | copy-start | bytes 1540
  164.6 53.5 %all-to-all-start.1 = ((f32[4,1,262144]{2,1,0:T(1,128)}), f32[4,1,262144]{2,1,0:T(1,128)}, u32[]{:S(2)}, u32[]{:S(2)}) async-start(f32[4,1,262144]{2,1,0:T(1,128)} %reshape.299), calls=%async_computation.1 | async-start | bytes 8388608 | tf_op jit(solution)/shard_map/all_to_all | solution.py:74
  263.2 63.5 %all-to-all-start.2 = ((f32[2,1,16,256,128]{4,2,0,1,3:T(8,128)}), f32[2,1,16,256,128]{4,2,0,1,3:T(8,128)}, u32[]{:S(2)}, u32[]{:S(2)}) async-start(f32[2,1,16,256,128]{4,2,0,1,3:T(8,128)} %copy.56), calls=%async_computation.2 | async-start | bytes 8388608 | tf_op jit(solution)/shard_map/all_to_all | solution.py:78
  329.4 7.2 %copy-start.2 = (f32[256,16,128]{2,1,0:T(8,128)S(1)}, f32[256,16,128]{2,1,0:T(8,128)}, u32[]{:S(2)}) copy-start(f32[256,16,128]{2,1,0:T(8,128)} %param.11) | copy-start | bytes 6291460
  329.4 7.2 %copy-start.3 = (f32[256,16,128]{2,1,0:T(8,128)S(1)}, f32[256,16,128]{2,1,0:T(8,128)}, u32[]{:S(2)}) copy-start(f32[256,16,128]{2,1,0:T(8,128)} %param.10) | copy-start | bytes 6291460
  424.1 53.7 %all-to-all-start.4 = ((f32[2,1,16,256,128]{4,2,0,1,3:T(8,128)}), f32[2,1,16,256,128]{4,2,0,1,3:T(8,128)}, u32[]{:S(2)}, u32[]{:S(2)}) async-start(f32[2,1,16,256,128]{4,2,0,1,3:T(8,128)} %copy.66), calls=%async_computation.4 | async-start | bytes 8388608 | tf_op jit(solution)/shard_map/all_to_all | solution.py:92
  490.1 9.9 %copy-start.1 = (f32[128,1024]{1,0:T(8,128)S(1)}, f32[128,1024]{1,0:T(8,128)}, u32[]{:S(2)}) copy-start(f32[128,1024]{1,0:T(8,128)} %param.6) | copy-start | bytes 1572868
